TPU v7x, 32 devices: a whole 2x2x4 slice. The times are simulated.
32 devices in a mesh: shard: 4 (over z), ctx: 4 (over y, x), tp: 2 (over core).
Axes of the slice: x: 2, y: 2, z: 4, core: 2. Of those that a mesh axis runs over, the one named last changes fastest.
Arguments:
- hidden_in: bfloat16 [24, 680, 1024], P('shard', 'ctx'), may hold values from -6 to 6
- cond: bfloat16 [24, 1024], P('shard'), may hold values from -6 to 6
- scale_len: int32 [24, 10], P('shard'), may hold values from 1 to 256, 680 in all within a row
- ada_weight: bfloat16 [1024, 6, 1024], P('shard'), may hold values from -0.1875 to 0.1875
- ada_bias: float32 [6, 1024], replicated, may hold values from -3 to 3
- qkv_weight: bfloat16 [1024, 3, 1024], P('shard', None, 'tp'), may hold values from -0.1875 to 0.1875
- query_bias: float32 [1024], P('tp'), may hold values from -3 to 3
- value_bias: float32 [1024], P('tp'), may hold values from -3 to 3
- head_scale: float32 [16], P('tp'), may hold values from 2 to 3
- proj_weight: bfloat16 [1024, 1024], P('tp', 'shard'), may hold values from -0.5 to 0.5
- proj_bias: float32 [1024], replicated, may hold values from -2 to 2
- up_weight: bfloat16 [1024, 4096], P('shard', 'tp'), may hold values from -0.1875 to 0.1875
- up_bias: float32 [4096], P('tp'), may hold values from -3 to 3
- down_weight: bfloat16 [4096, 1024], P('tp', 'shard'), may hold values from -0.125 to 0.125
- down_bias: float32 [1024], replicated, may hold values from -2 to 2
- out_grad: bfloat16 [24, 680, 1024], P('shard', 'ctx'), may hold values from -6 to 6
Outputs:
- hidden_out: bfloat16 [24, 680, 1024], P('shard', 'ctx')
- grad_hidden: bfloat16 [24, 680, 1024], P('shard', 'ctx')
- grad_cond: float32 [24, 1024], P('shard')
- grad_ada_weight: float32 [1024, 6, 1024], P('shard')
- grad_ada_bias: float32 [6, 1024], replicated
- grad_qkv_weight: float32 [1024, 3, 1024], P('shard', None, 'tp')
- grad_query_bias: float32 [1024], P('tp')
- grad_value_bias: float32 [1024], P('tp')
- grad_head_scale: float32 [16], P('tp')
- grad_proj_weight: float32 [1024, 1024], P('tp', 'shard')
- grad_proj_bias: float32 [1024], replicated
- grad_up_weight: float32 [1024, 4096], P('shard', 'tp')
- grad_up_bias: float32 [4096], P('tp')
- grad_down_weight: float32 [4096, 1024], P('tp', 'shard')
- grad_down_bias: float32 [1024], replicated
- norm_stats: float32 [3], replicated
Inputs may be any that keep to these rules, and one draw needn't show every extreme that they name: `scale_len`: each row holds the token counts of one map's 10 scales in order; they sum to 680, and the largest in every row is 256.
All inputs are finite; a program needn't handle non-finite values.
Results may differ from a plain program's by a relative error of at most 0.03.
Values may be sent and summed in bfloat16 or wider, within the bound.
No kernel may reach another device: no remote copies, remote signals or barrier semaphores. Data moves between devices by JAX's collectives and lax.ppermute only.
A program may use at most 256 MiB of HBM per device.

v0:
```python
import jax
import jax.numpy as jnp
from jax import lax
from jax.sharding import PartitionSpec as P


def layer_norm(values):
    center = values - jnp.mean(values, axis=-1, keepdims=True)
    spread = jnp.mean(center * center, axis=-1, keepdims=True)
    return center * lax.rsqrt(spread + 1e-06)


def modulate(values, scale, shift):
    return layer_norm(values) * (1.0 + scale[:, None, :]) + shift[:, None, :]


def unit_scaled(values, gains):
    normed = values * lax.rsqrt(jnp.sum(values * values, axis=-1, keepdims=True) + 1e-06)
    return normed * jnp.exp(gains)[None, None, :, None]


def unit_plain(values):
    return values * lax.rsqrt(jnp.sum(values * values, axis=-1, keepdims=True) + 1e-06)


def gelu_tanh(values):
    return jax.nn.gelu(values, approximate=True)


def tp_sum(values):
    count = lax.axis_size("tp")
    if count != 2:
        return lax.psum(values, "tp")
    return values + lax.ppermute(values, "tp", [(0, 1), (1, 0)])


def ctx_shifts(values):
    count = lax.axis_size("ctx")
    parts = [values]
    for shift in range(1, count):
        pairs = [(i, (i + shift) % count) for i in range(count)]
        parts.append(lax.ppermute(values, "ctx", pairs))
    return jnp.stack(parts)


def ctx_return(parts):
    count = lax.axis_size("ctx")
    total = parts[0].astype(jnp.float32)
    for shift in range(1, count):
        pairs = [(i, (i - shift) % count) for i in range(count)]
        total = total + lax.ppermute(parts[shift], "ctx", pairs).astype(jnp.float32)
    return total


def body(
    hidden_in,
    cond,
    scale_len,
    ada_weight,
    ada_bias,
    qkv_weight,
    query_bias,
    value_bias,
    head_scale,
    proj_weight,
    proj_bias,
    up_weight,
    up_bias,
    down_weight,
    down_bias,
    out_grad,
):
    map_count = hidden_in.shape[0]
    piece_rows = hidden_in.shape[1]
    model_width = hidden_in.shape[2]
    ctx_count = lax.axis_size("ctx")
    ctx_index = lax.axis_index("ctx")
    shard_index = lax.axis_index("shard")
    map_length = piece_rows * ctx_count
    heads_here = head_scale.shape[0]
    local_width = query_bias.shape[0]
    head_dim = local_width // heads_here
    row_count = map_count * piece_rows
    head_shape = (map_count, piece_rows, heads_here, head_dim)
    ada_rows = ada_weight.shape[0]
    full_qkv, full_up, full_proj, full_down = (
        lax.all_gather(qkv_weight, "shard", axis=0, tiled=True),
        lax.all_gather(up_weight, "shard", axis=0, tiled=True),
        lax.all_gather(proj_weight, "shard", axis=1, tiled=True),
        lax.all_gather(down_weight, "shard", axis=1, tiled=True),
    )
    qkv_matrix = full_qkv.reshape(model_width, 3 * local_width)
    cond_wide = cond.astype(jnp.float32)
    cond_all = lax.all_gather(cond, "shard", axis=0, tiled=True).astype(jnp.float32)
    cond_in_all = jax.nn.silu(cond_all).astype(jnp.bfloat16)
    cond_cols = lax.dynamic_slice_in_dim(cond_in_all, shard_index * ada_rows, ada_rows, axis=1)
    ada_local = ada_weight.reshape(ada_rows, 6 * model_width)
    mod_partial = jnp.dot(cond_cols, ada_local, preferred_element_type=jnp.float32)
    modulation = lax.psum_scatter(mod_partial, "shard", scatter_dimension=0, tiled=True)
    modulation = modulation.reshape(map_count, 6, model_width) + ada_bias[None]
    gamma_one = modulation[:, 0]
    gamma_two = modulation[:, 1]
    scale_one = modulation[:, 2]
    scale_two = modulation[:, 3]
    shift_one = modulation[:, 4]
    shift_two = modulation[:, 5]
    stream_in = hidden_in.astype(jnp.float32)
    first_mod, first_back = jax.vjp(modulate, stream_in, scale_one, shift_one)
    attn_in = first_mod.astype(jnp.bfloat16).reshape(row_count, model_width)
    qkv = jnp.dot(attn_in, qkv_matrix, preferred_element_type=jnp.float32).reshape(
        map_count, piece_rows, 3, local_width
    )
    query = (qkv[:, :, 0] + query_bias).reshape(head_shape)
    key_raw = qkv[:, :, 1].reshape(head_shape)
    value_low = (qkv[:, :, 2] + value_bias).astype(jnp.bfloat16).reshape(head_shape)
    query_unit, query_back = jax.vjp(unit_scaled, query, head_scale)
    key_unit, key_back = jax.vjp(unit_plain, key_raw)
    query_low = query_unit.astype(jnp.bfloat16)
    key_low = key_unit.astype(jnp.bfloat16)
    keys_parts = ctx_shifts(key_low)
    values_parts = ctx_shifts(value_low)
    scale_ends = jnp.cumsum(scale_len, axis=1)
    query_pos = ctx_index * piece_rows + jnp.arange(piece_rows, dtype=jnp.int32)
    visible_end = jnp.min(
        jnp.where(
            scale_ends[:, None, :] > query_pos[None, :, None], scale_ends[:, None, :], map_length
        ),
        axis=2,
    )
    owners = (ctx_index - jnp.arange(ctx_count, dtype=jnp.int32)) % ctx_count
    key_pos = owners[:, None] * piece_rows + jnp.arange(piece_rows, dtype=jnp.int32)[None, :]
    key_mask = key_pos[None, None, :, :] < visible_end[:, :, None, None]

    def masked_scores():
        raw_scores = jnp.einsum(
            "mqhd,nmkhd->mhqnk", query_low, keys_parts, preferred_element_type=jnp.float32
        )
        return jnp.where(key_mask[:, None], raw_scores, -1e30)

    scores = masked_scores()
    row_max = jnp.max(scores, axis=(-2, -1), keepdims=True)
    exp_scores = jnp.exp(scores - row_max)
    exp_total = jnp.sum(exp_scores, axis=(-2, -1), keepdims=True)
    log_total = row_max + jnp.log(exp_total)
    probs_low = (exp_scores / exp_total).astype(jnp.bfloat16)
    heads_out = jnp.einsum(
        "mhqnk,nmkhd->mqhd", probs_low, values_parts, preferred_element_type=jnp.float32
    )
    heads_out = heads_out.reshape(row_count, local_width).astype(jnp.bfloat16)
    attn_partial = jnp.dot(heads_out, full_proj, preferred_element_type=jnp.float32)
    attn_branch = tp_sum(attn_partial).reshape(map_count, piece_rows, model_width) + proj_bias
    attn_part = gamma_one[:, None] * attn_branch
    mid_stream = stream_in + attn_part
    second_mod, second_back = jax.vjp(modulate, mid_stream, scale_two, shift_two)
    mlp_in = second_mod.astype(jnp.bfloat16).reshape(row_count, model_width)
    pre_act = jnp.dot(mlp_in, full_up, preferred_element_type=jnp.float32) + up_bias
    activation, gelu_back = jax.vjp(gelu_tanh, pre_act)
    act_low = activation.astype(jnp.bfloat16)
    mlp_partial = jnp.dot(act_low, full_down, preferred_element_type=jnp.float32)
    mlp_branch = tp_sum(mlp_partial).reshape(map_count, piece_rows, model_width) + down_bias
    mlp_part = gamma_two[:, None] * mlp_branch
    stream = mid_stream + mlp_part
    grad_top = out_grad.astype(jnp.float32)
    d_gamma_two = jnp.sum(grad_top * mlp_branch, axis=1)
    d_mlp = gamma_two[:, None] * grad_top
    d_down_bias = jnp.sum(d_mlp, axis=(0, 1))
    d_mlp_low = d_mlp.astype(jnp.bfloat16).reshape(row_count, model_width)
    g_down = jnp.einsum("rf,rd->fd", act_low, d_mlp_low, preferred_element_type=jnp.float32)
    d_act = jnp.einsum("rd,fd->rf", d_mlp_low, full_down, preferred_element_type=jnp.float32)
    (d_pre,) = gelu_back(d_act)
    d_up_bias = jnp.sum(d_pre, axis=0)
    d_pre_low = d_pre.astype(jnp.bfloat16)
    g_up = jnp.einsum("rd,rf->df", mlp_in, d_pre_low, preferred_element_type=jnp.float32)
    d_mlp_in_part = jnp.einsum("rf,df->rd", d_pre_low, full_up, preferred_element_type=jnp.float32)
    d_mlp_in = tp_sum(d_mlp_in_part).reshape(map_count, piece_rows, model_width)
    d_mid, d_scale_two, d_shift_two = second_back(d_mlp_in)
    d_mid = d_mid + grad_top
    d_gamma_one = jnp.sum(d_mid * attn_branch, axis=1)
    d_attn = gamma_one[:, None] * d_mid
    d_proj_bias = jnp.sum(d_attn, axis=(0, 1))
    d_attn_low = d_attn.astype(jnp.bfloat16).reshape(row_count, model_width)
    g_proj = jnp.einsum("ri,rd->id", heads_out, d_attn_low, preferred_element_type=jnp.float32)
    d_heads = jnp.einsum("rd,id->ri", d_attn_low, full_proj, preferred_element_type=jnp.float32)
    d_heads = d_heads.astype(jnp.bfloat16).reshape(head_shape)
    probs = jnp.exp(masked_scores() - log_total)
    d_probs = jnp.einsum(
        "mqhd,nmkhd->mhqnk", d_heads, values_parts, preferred_element_type=jnp.float32
    )
    row_delta = jnp.sum(probs * d_probs, axis=(-2, -1), keepdims=True)
    d_scores = (probs * (d_probs - row_delta)).astype(jnp.bfloat16)
    d_query_unit = jnp.einsum(
        "mhqnk,nmkhd->mqhd", d_scores, keys_parts, preferred_element_type=jnp.float32
    )
    probs_again = probs.astype(jnp.bfloat16)
    d_key_parts = jnp.einsum(
        "mhqnk,mqhd->nmkhd", d_scores, query_low, preferred_element_type=jnp.float32
    ).astype(jnp.bfloat16)
    d_value_parts = jnp.einsum(
        "mhqnk,mqhd->nmkhd", probs_again, d_heads, preferred_element_type=jnp.float32
    ).astype(jnp.bfloat16)
    d_key_unit = ctx_return(d_key_parts)
    d_value = ctx_return(d_value_parts)
    d_query, d_head_scale = query_back(d_query_unit)
    (d_key,) = key_back(d_key_unit)
    d_query = d_query.reshape(map_count, piece_rows, local_width)
    d_key = d_key.reshape(map_count, piece_rows, local_width)
    d_value = d_value.reshape(map_count, piece_rows, local_width)
    d_query_bias = jnp.sum(d_query, axis=(0, 1))
    d_value_bias = jnp.sum(d_value, axis=(0, 1))
    d_qkv = (
        jnp.stack([d_query, d_key, d_value], axis=2)
        .astype(jnp.bfloat16)
        .reshape(row_count, 3 * local_width)
    )
    g_qkv = jnp.einsum("rd,rc->dc", attn_in, d_qkv, preferred_element_type=jnp.float32).reshape(
        model_width, 3, local_width
    )
    d_attn_in_part = jnp.einsum("rc,dc->rd", d_qkv, qkv_matrix, preferred_element_type=jnp.float32)
    d_attn_in = tp_sum(d_attn_in_part).reshape(map_count, piece_rows, model_width)
    d_input, d_scale_one, d_shift_one = first_back(d_attn_in)
    d_input = d_input + d_mid
    d_mod_part = jnp.stack(
        [d_gamma_one, d_gamma_two, d_scale_one, d_scale_two, d_shift_one, d_shift_two], axis=1
    )
    d_mod = lax.psum(d_mod_part, "ctx").astype(jnp.bfloat16).reshape(map_count, 6 * model_width)
    d_mod_all = lax.all_gather(d_mod, "shard", axis=0, tiled=True)
    g_ada = jnp.einsum(
        "md,mc->dc", cond_cols, d_mod_all, preferred_element_type=jnp.float32
    ).reshape(ada_rows, 6, model_width)
    d_ada_bias = jnp.sum(d_mod_all.astype(jnp.float32), axis=0).reshape(6, model_width)
    d_cond_cols = jnp.einsum("mc,dc->md", d_mod_all, ada_local, preferred_element_type=jnp.float32)
    d_cond_in = lax.all_to_all(d_cond_cols, "shard", 0, 1, tiled=True)
    silu_value, silu_back = jax.vjp(jax.nn.silu, cond_wide)
    (d_cond,) = silu_back(d_cond_in)
    shard_grads = (
        lax.psum_scatter(g_qkv.astype(jnp.bfloat16), "shard", scatter_dimension=0, tiled=True),
        lax.psum_scatter(g_up.astype(jnp.bfloat16), "shard", scatter_dimension=0, tiled=True),
        lax.psum_scatter(g_proj.astype(jnp.bfloat16), "shard", scatter_dimension=1, tiled=True),
        lax.psum_scatter(g_down.astype(jnp.bfloat16), "shard", scatter_dimension=1, tiled=True),
    )
    summed = tuple((lax.psum(g, "ctx").astype(jnp.float32) for g in shard_grads))
    square_sums = jnp.stack(
        [jnp.sum(stream * stream), jnp.sum(attn_part * attn_part), jnp.sum(mlp_part * mlp_part)]
    )
    small_parts = (
        square_sums,
        d_query_bias,
        d_value_bias,
        d_head_scale,
        d_proj_bias,
        d_up_bias,
        d_down_bias,
    )
    small_flat = lax.psum(jnp.concatenate(small_parts), ("shard", "ctx"))
    small = []
    offset = 0
    for part in small_parts:
        small.append(small_flat[offset : offset + part.shape[0]])
        offset += part.shape[0]
    entry_total = map_count * map_length * model_width * lax.axis_size("shard")
    norm_stats = jnp.sqrt(small[0] / entry_total)
    return (
        stream.astype(jnp.bfloat16),
        d_input.astype(jnp.bfloat16),
        d_cond,
        g_ada,
        d_ada_bias,
        summed[0],
        small[1],
        small[2],
        small[3],
        summed[2],
        small[4],
        summed[1],
        small[5],
        summed[3],
        small[6],
        norm_stats,
    )


def solution(mesh):
    in_specs = (
        P("shard", "ctx", None),
        P("shard", None),
        P("shard", None),
        P("shard", None, None),
        P(),
        P("shard", None, "tp"),
        P("tp"),
        P("tp"),
        P("tp"),
        P("tp", "shard"),
        P(),
        P("shard", "tp"),
        P("tp"),
        P("tp", "shard"),
        P(),
        P("shard", "ctx", None),
    )
    out_specs = (
        P("shard", "ctx", None),
        P("shard", "ctx", None),
        P("shard", None),
        P("shard", None, None),
        P(),
        P("shard", None, "tp"),
        P("tp"),
        P("tp"),
        P("tp"),
        P("tp", "shard"),
        P(),
        P("shard", "tp"),
        P("tp"),
        P("tp", "shard"),
        P(),
        P(),
    )
    return jax.shard_map(body, mesh=mesh, in_specs=in_specs, out_specs=out_specs, check_vma=False)
```

profile of v0, /device:TPU:0, one launch (start us, length us, event | category | flops | bytes accessed | tf_op | source)
XLA Modules:
  0.0 946.9 jit_solution(184470483697342123)
XLA Ops:
  10.3 15.2 %all-gather = bf16[4,6,1024]{2,1,0:T(8,128)(2,1)S(1)} all-gather(bf16[1,6,1024]{2,1,0:T(8,128)(2,1)} %bitcast.222), channel_id=1, replica_groups=mesh['shard'=4,'ctx'=4,'tp'=2] {'shard'}, dimensions={0}, use_global_device_ids=true | all-gather | bytes 61440 | tf_op jit(solution)/shard_map/all_gather | solution.py:94
  33.2 36.0 %fusion = f32[8,6144]{1,0:T(8,128)S(1)} fusion(f32[24,6144]{1,0:T(8,128)S(1)} %fusion.72), kind=kCustom, calls=%all-reduce-scatter | all-reduce-scatter fusion | flops 196609 | bytes 786944
  84.2 5.2 all-gather.7.cloned.1.call-done
  89.3 6.1 fusion.39
  124.1 49.5 %collective-permute-done.5 = bf16[6,170,8,64]{1,3,2,0:T(8,128)(2,1)} collective-permute-done((bf16[6,170,8,64]{1,3,2,0:T(8,128)(2,1)}, bf16[6,170,8,64]{1,3,2,0:T(8,128)(2,1)}, u32[]{:S(2)}, u32[]{:S(2)}) %collective-permute-start.5) | collective-permute-done | bytes 1044512 | tf_op jit(solution)/shard_map/ppermute | solution.py:42
  176.1 65.5 %collective-permute-done.4 = bf16[6,170,8,64]{1,3,2,0:T(8,128)(2,1)} collective-permute-done((bf16[6,170,8,64]{1,3,2,0:T(8,128)(2,1)}, bf16[6,170,8,64]{1,3,2,0:T(8,128)(2,1)}, u32[]{:S(2)}, u32[]{:S(2)}) %collective-permute-start.4) | collective-permute-done | bytes 1044512 | tf_op jit(solution)/shard_map/ppermute | solution.py:42
  241.7 17.0 %select_reduce_fusion = (f32[6,8,170]{2,1,0:T(8,128)S(1)}, f32[6,8,170,4,170]{2,4,3,1,0:T(8,128)}) fusion(pred[6,170,4,170]{1,3,2,0:T(8,128)(4,1)} %broadcast_compare_fusion, bf16[1,6,170,8,64]{2,4,0,3,1:T(8,128)(2,1)} %bitcast.26, bf16[1,6,170,8,64]{2,4,0,3,1:T(8,128)(2,1)} %bitcast.25, bf16[1,6,170,8,64]{2,4,0,3,1:T(8,128)(2,1)} %bitcast.23, ...), kind=kOutput, calls=%fused_computation.6 | convolution fusion | flops 740136448 | bytes 29223040 | tf_op jit(solution)/shard_map/mqhd,nmkhd->mhqnk/dot_general | solution.py:135
  258.7 14.9 %fusion.1 = f32[6,8,170]{2,1,0:T(8,128)S(1)} fusion(f32[6,8,170,4,170]{2,4,3,1,0:T(8,128)} %get-tuple-element.133, f32[6,8,170]{2,1,0:T(8,128)S(1)} %get-tuple-element.132, pred[6,170,4,170]{1,3,2,0:T(8,128)(4,1)S(1)} %copy-done.11), kind=kLoop, calls=%fused_computation.5 | loop fusion | flops 16638240 | bytes 22954080 | tf_op jit(solution)/shard_map/reduce_sum | solution.py:143
  273.6 18.0 %fusion.51 = bf16[6,170,8,64]{1,3,2,0:T(8,128)(2,1)} fusion(f32[6,8,170,4,170]{2,4,3,1,0:T(8,128)} %get-tuple-element.133, f32[6,8,170]{2,1,0:T(8,128)S(1)} %fusion.1, f32[6,8,170]{2,1,0:T(8,128)S(1)} %get-tuple-element.132, pred[6,170,4,170]{1,3,2,0:T(8,128)(4,1)S(1)} %copy-done.11, bf16[1,6,170,8,64]{2,4,0,3,1:T(8,128)(2,1)} %bitcast.15, ...), kind=kOutput, calls=%fused_computation.109 | convolution fusion | flops 739230720 | bytes 28176480 | tf_op jit(solution)/shard_map/mhqnk,nmkhd->mqhd/dot_general | solution.py:146
  291.7 12.4 %copy.134 = bf16[6,170,8,64]{3,2,1,0:T(8,128)(2,1)S(1)} copy(bf16[6,170,8,64]{1,3,2,0:T(8,128)(2,1)} %fusion.51) | data formatting | bytes 2088960 | tf_op jit(solution)/shard_map/convert_element_type | solution.py:149
  306.4 5.0 fusion.85
  323.7 9.5 multiply_reduce_fusion.7
  346.3 10.8 %fusion.86 = f32[1020,2048]{1,0:T(8,128)} fusion(bf16[1020,1024]{1,0:T(8,128)(2,1)} %reshape.313, bf16[1024,2048]{1,0:T(8,128)(2,1)} %all-gather.11.cloned.1.call-done), kind=kOutput, calls=%fused_computation.178 | convolution fusion | flops 4278190080 | bytes 14639104 | tf_op jit(solution)/shard_map/dot_general | solution.py:156
  357.1 35.6 %all-gather.13.cloned.1.call-done = bf16[2048,1024]{1,0:T(8,128)(2,1)} async-done(((bf16[2048,256]{1,0:T(8,128)(2,1)}), bf16[2048,1024]{1,0:T(8,128)(2,1)}) %all-gather.13.cloned.1.call-update) | async-done | bytes 4194320 | tf_op jit(solution)/shard_map/all_gather | solution.py:90
  392.7 14.2 %fusion.76 = (f32[2048]{0:T(1024)}, bf16[1020,2048]{1,0:T(8,128)(2,1)S(1)}) fusion(f32[1020,2048]{1,0:T(8,128)} %fusion.86, f32[2048]{0:T(1024)S(1)} %copy-done.58, bf16[1020,1024]{1,0:T(8,128)(2,1)S(1)} %copy-done.18, bf16[2048,1024]{1,0:T(8,128)(2,1)} %all-gather.13.cloned.1.call-done), kind=kOutput, calls=%fused_computation.170 | convolution fusion | flops 4324145152 | bytes 18833408 | tf_op jit(solution)/shard_map/rd,fd->rf/dot_general | solution.py:169
  406.9 6.2 fusion.45
  414.6 7.0 fusion.74
  428.3 6.9 add.315
  439.3 9.3 multiply_reduce_fusion.6
  452.9 8.9 multiply_reduce_fusion.1
  466.0 5.2 multiply_reduce_fusion.8
  480.2 8.3 convolution_convert_fusion.1
  491.9 12.7 %convolution_convert_fusion = bf16[2048,1024]{1,0:T(8,128)(2,1)} fusion(bf16[1020,1024]{1,0:T(8,128)(2,1)} %reshape.315, f32[1020,2048]{1,0:T(8,128)} %fusion.86, f32[2048]{0:T(1024)S(1)} %copy-done.58), kind=kOutput, calls=%fused_computation.65 | convolution fusion | flops 4301176832 | bytes 14647296 | tf_op jit(solution)/shard_map/rf,rd->fd/dot_general | solution.py:168
  516.6 16.9 %convert_bitcast_fusion = bf16[4,6,170,8,64]{2,4,0,3,1:T(8,128)(2,1)} fusion(bf16[6,170,8,64,1]{1,3,4,2,0:T(8,128)(2,1)S(1)} %copy.156, f32[6,8,170,4,170]{2,4,3,1,0:T(8,128)} %get-tuple-element.133, f32[6,8,170]{2,1,0:T(8,128)S(1)} %log_add_fusion, pred[6,170,4,170]{1,3,2,0:T(8,128)(4,1)S(1)} %copy-done.11), kind=kOutput, calls=%fused_computation.39 | convolution fusion | flops 728981760 | bytes 28143840 | tf_op jit(solution)/shard_map/mhqnk,mqhd->nmkhd/dot_general | solution.py:198
  533.4 29.0 %multiply_reduce_fusion = (f32[6,8,170]{2,1,0:T(8,128)S(1)}, f32[6,8,170,4,170]{2,4,3,1,0:T(8,128)}) fusion(f32[6,8,170,4,170]{2,4,3,1,0:T(8,128)} %get-tuple-element.133, f32[6,8,170]{2,1,0:T(8,128)S(1)} %log_add_fusion, pred[6,170,4,170]{1,3,2,0:T(8,128)(4,1)S(1)} %copy-done.11, bf16[6,170,8,64,1]{1,3,4,2,0:T(8,128)(2,1)S(1)} %copy.156, ...), kind=kOutput, calls=%fused_computation.1 | convolution fusion | flops 749145088 | bytes 50371680 | tf_op jit(solution)/shard_map/mqhd,nmkhd->mhqnk/dot_general | solution.py:186
  562.4 4.7 slice_bitcast_fusion.2
  570.7 29.9 %multiply_convert_fusion = bf16[6,8,170,4,170]{2,4,3,1,0:T(8,128)(2,1)} fusion(f32[6,8,170,4,170]{2,4,3,1,0:T(8,128)} %get-tuple-element.135, f32[6,8,170,4,170]{2,4,3,1,0:T(8,128)} %get-tuple-element.133, f32[6,8,170]{2,1,0:T(8,128)S(1)} %get-tuple-element.134, f32[6,8,170]{2,1,0:T(8,128)S(1)} %log_add_fusion, pred[6,170,4,170]{1,3,2,0:T(8,128)(4,1)} %broadcast_compare_fusion), kind=kLoop, calls=%fused_computation | loop fusion | flops 27744000 | bytes 56246880 | tf_op jit(solution)/shard_map/convert_element_type | solution.py:190
  600.6 11.2 %convert_bitcast_fusion.1 = bf16[4,6,170,8,64]{2,4,3,1,0:T(8,128)(2,1)} fusion(bf16[6,8,170,4,170]{2,4,3,1,0:T(8,128)(2,1)} %multiply_convert_fusion, f32[6,170,8,64]{1,3,2,0:T(8,128)S(1)} %bitcast.187, f32[8]{0:T(128)S(1)} %copy-done.52, f32[6,170,8]{1,2,0:T(8,128)S(1)} %copy-done.31, f32[8,64]{1,0:T(8,128)S(1)} %copy-done.44), kind=kOutput, calls=%fused_computation.40 | convolution fusion | flops 714424320 | bytes 17399200 | tf_op jit(solution)/shard_map/mhqnk,mqhd->nmkhd/dot_general | solution.py:195
  611.8 4.8 slice_bitcast_fusion.6
  620.7 9.6 %fusion.41 = (f32[8]{0:T(128)S(1)}, f32[6,170,8]{1,2,0:T(8,128)S(1)}, f32[6,8,64,170,1]{3,2,4,1,0:T(8,128)S(1)}) fusion(f32[6,170,8,64]{1,3,2,0:T(8,128)S(1)} %bitcast.188, f32[6,170,8]{1,2,0:T(8,128)S(1)} %copy-done.31, f32[8,64]{1,0:T(8,128)S(1)} %copy-done.44, f32[8]{0:T(128)S(1)} %copy-done.52, bf16[6,8,170,4,170]{2,4,3,1,0:T(8,128)(2,1)} %multiply_convert_fusion, ...), kind=kOutput, calls=%fused_computation.77 | convolution fusion | flops 720160768 | bytes 19520832 | tf_op jit(solution)/shard_map/mhqnk,nmkhd->mqhd/dot_general | solution.py:191
  630.4 9.0 collective-permute-done.14
  640.8 5.0 fusion.78
  645.8 6.4 copy.146
  652.2 6.3 copy.144
  658.5 13.7 %collective-permute-done.9 = bf16[6,170,8,64]{1,3,2,0:T(8,128)(2,1)} collective-permute-done((bf16[6,170,8,64]{1,3,2,0:T(8,128)(2,1)}, bf16[6,170,8,64]{1,3,2,0:T(8,128)(2,1)}, u32[]{:S(2)}, u32[]{:S(2)}) %collective-permute-start.9) | collective-permute-done | bytes 1044512 | tf_op jit(solution)/shard_map/ppermute | solution.py:51
  672.1 34.4 %collective-permute-done.11 = bf16[6,170,8,64]{1,3,2,0:T(8,128)(2,1)} collective-permute-done((bf16[6,170,8,64]{1,3,2,0:T(8,128)(2,1)}, bf16[6,170,8,64]{1,3,2,0:T(8,128)(2,1)}, u32[]{:S(2)}, u32[]{:S(2)}) %collective-permute-start.11) | collective-permute-done | bytes 1044512 | tf_op jit(solution)/shard_map/ppermute | solution.py:51
  711.9 5.7 add_add_fusion.2
  717.7 6.4 copy.145
  724.1 8.3 maximum_convert_fusion
  738.2 7.7 convolution_convert_fusion.2
  746.0 6.8 fusion.87
  755.2 75.6 %psum.44 = f32[5131]{0:T(1024)S(1)} all-reduce(f32[5131]{0:T(1024)S(1)} %concatenate.3), channel_id=1, replica_groups=mesh['shard'=4,'ctx'=4,'tp'=2] {'shard','ctx'}, use_global_device_ids=true, to_apply=%region_37.38 | all-reduce | flops 5131 | bytes 41048 | tf_op jit(solution)/shard_map/psum | solution.py:254
  833.9 6.8 add.323
  852.0 20.3 %all-reduce.7 = bf16[6,6,1024]{2,1,0:T(8,128)(2,1)S(1)} all-reduce(f32[6,6,1024]{2,1,0:T(8,128)S(1)} %stack.61), channel_id=1, replica_groups=mesh['shard'=4,'ctx'=4,'tp'=2] {'ctx'}, use_global_device_ids=true, to_apply=%region_24.25 | all-reduce | flops 36864 | bytes 221184 | tf_op jit(solution)/shard_map/psum | solution.py:225
  872.5 14.2 %all-gather.1 = bf16[4,6,6144]{2,1,0:T(8,128)(2,1)S(1)} all-gather(bf16[1,6,6144]{2,1,0:T(8,128)(2,1)S(1)} %reshape.332), channel_id=1, replica_groups=mesh['shard'=4,'ctx'=4,'tp'=2] {'shard'}, dimensions={0}, use_global_device_ids=true | all-gather | bytes 368640 | tf_op jit(solution)/shard_map/all_gather | solution.py:226
  898.0 5.3 add_convert_fusion
  904.0 6.6 copy.151
  911.2 20.1 %all-reduce.6.cloned.1.call-done = (bf16[256,3,512]{2,0,1:T(8,128)(2,1)}, bf16[512,256]{1,0:T(8,128)(2,1)}, bf16[256,2048]{1,0:T(8,128)(2,1)}, bf16[2048,256]{1,0:T(8,128)(2,1)}) async-done(((bf16[256,3,512]{2,0,1:T(8,128)(2,1)}, bf16[512,256]{1,0:T(8,128)(2,1)}, bf16[256,2048]{1,0:T(8,128)(2,1)}, bf16[2048,256]{1,0:T(8,128)(2,1)}), (bf16[256,3,512]{2,0,1:T(8,128)(2,1)}, bf16[512,256]{1,0:T(8,128)(2,1)}, ...) | async-done | bytes 3145744 | tf_op jit(solution)/shard_map/psum | solution.py:241
  (295 shorter events, 186.9 us)
Async XLA Ops:
  7.2 82.1 %all-gather.7.cloned.1.call-start = ((), (), s32[]{:S(2)}) async-start(), calls=%async_computation.5 | async-start | bytes 3932160 | tf_op jit(solution)/shard_map/all_gather | solution.py:87
  9.5 296.8 %all-gather.9.cloned.1.call-start = ((), (), s32[]{:S(2)}) async-start(), calls=%async_computation.6 | async-start | bytes 1310720 | tf_op jit(solution)/shard_map/all_gather | solution.py:89
  10.3 336.1 %all-gather.11.cloned.1.call-start = ((), (), s32[]{:S(2)}) async-start(), calls=%async_computation.7 | async-start | bytes 5242880 | tf_op jit(solution)/shard_map/all_gather | solution.py:88
  30.2 42.3 %copy-start.59 = (f32[8]{0:T(128)S(1)}, f32[8]{0:T(128)}, u32[]{:S(2)}) copy-start(f32[8]{0:T(128)} %param.24) | copy-start | bytes 100
  30.2 42.4 %copy-start.53 = (f32[512]{0:T(512)S(1)}, f32[512]{0:T(512)}, u32[]{:S(2)}) copy-start(f32[512]{0:T(512)} %param.22) | copy-start | bytes 6148
  30.2 42.5 %copy-start.54 = (f32[512]{0:T(512)S(1)}, f32[512]{0:T(512)}, u32[]{:S(2)}) copy-start(f32[512]{0:T(512)} %param.23) | copy-start | bytes 6148
  30.2 42.6 %copy-start.50 = (s32[6,10]{1,0:T(8,128)S(1)}, s32[6,10]{1,0:T(8,128)}, u32[]{:S(2)}) copy-start(s32[6,10]{1,0:T(8,128)} %param.18) | copy-start | bytes 724
  30.3 42.8 %copy-start.3 = (bf16[6,170,1024]{2,1,0:T(8,128)(2,1)S(1)}, bf16[6,170,1024]{2,1,0:T(8,128)(2,1)}, u32[]{:S(2)}) copy-start(bf16[6,170,1024]{2,1,0:T(8,128)(2,1)} %param.16) | copy-start | bytes 6266884
  33.2 41.0 %copy-start.55 = (u32[32]{0:T(128)S(1)}, u32[32]{0:T(128)}, u32[]{:S(2)}) copy-start(u32[32]{0:T(128)} %constant.87) | copy-start | bytes 388
  69.3 10.3 %collective-permute-start.16 = (f32[6,6144]{1,0:T(8,128)S(1)}, f32[6,6144]{1,0:T(8,128)S(1)}, u32[]{:S(2)}, u32[]{:S(2)}) collective-permute-start(f32[6,6144]{1,0:T(8,128)S(1)} %slice.120), channel_id=1, source_target_pairs={{0,8},{8,16},{16,24},{1,9},{9,17},{17,25},{2,10},{10,18},{18,26},{... | collective-permute-start | bytes 442376
  72.4 320.3 %all-gather.13.cloned.1.call-start = ((), (), s32[]{:S(2)}) async-start(), calls=%async_computation.8 | async-start | bytes 5242880 | tf_op jit(solution)/shard_map/all_gather | solution.py:90
  72.5 169.1 %copy-start.51 = (f32[8]{0:T(128)}, f32[8]{0:T(128)S(1)}, u32[]{:S(2)}) copy-start(f32[8]{0:T(128)S(1)} %exp.18) | copy-start | bytes 100
  72.7 168.9 %copy-start.43 = (f32[8,64]{1,0:T(8,128)}, f32[8,64]{1,0:T(8,128)S(1)}, u32[]{:S(2)}) copy-start(f32[8,64]{1,0:T(8,128)S(1)} %add.292) | copy-start | bytes 6148
  77.2 18.2 %copy-start.35 = (f32[6,170]{1,0:T(8,128)}, f32[6,170]{1,0:T(8,128)S(1)}, u32[]{:S(2)}) copy-start(f32[6,170]{1,0:T(8,128)S(1)} %fusion.61) | copy-start | bytes 12244
  102.3 171.3 %collective-permute-start.2 = (bf16[6,170,8,64]{1,3,2,0:T(8,128)(2,1)}, bf16[6,170,8,64]{1,3,2,0:T(8,128)(2,1)}, u32[]{:S(2)}, u32[]{:S(2)}) collective-permute-start(bf16[6,170,8,64]{1,3,2,0:T(8,128)(2,1)} %add_convert_fusion.2), channel_id=1, source_target_pairs={{0,6},{2,0},{4,2},{6,4},{1,7},{3,1},{5,3},{7,5},{8,14},{10,8},{12,... | collective-permute-start | bytes 3133448 | tf_op jit(solution)/shard_map/ppermute | solution.py:42
  104.9 168.8 %collective-permute-start.1 = (bf16[6,170,8,64]{1,3,2,0:T(8,128)(2,1)}, bf16[6,170,8,64]{1,3,2,0:T(8,128)(2,1)}, u32[]{:S(2)}, u32[]{:S(2)}) collective-permute-start(bf16[6,170,8,64]{1,3,2,0:T(8,128)(2,1)} %add_convert_fusion.2), channel_id=1, source_target_pairs={{0,4},{2,6},{4,0},{6,2},{1,5},{3,7},{5,1},{7,3},{8,12},{10,14},{12... | collective-permute-start | bytes 3133448 | tf_op jit(solution)/shard_map/ppermute | solution.py:42
  110.6 63.1 %collective-permute-start.5 = (bf16[6,170,8,64]{1,3,2,0:T(8,128)(2,1)}, bf16[6,170,8,64]{1,3,2,0:T(8,128)(2,1)}, u32[]{:S(2)}, u32[]{:S(2)}) collective-permute-start(bf16[6,170,8,64]{1,3,2,0:T(8,128)(2,1)} %multiply_convert_fusion.3), channel_id=1, source_target_pairs={{0,6},{2,0},{4,2},{6,4},{1,7},{3,1},{5,3},{7,5},{8,14},{10,8},{12,... | collective-permute-start | bytes 3133448 | tf_op jit(solution)/shard_map/ppermute | solution.py:42
  111.1 130.6 %collective-permute-start.4 = (bf16[6,170,8,64]{1,3,2,0:T(8,128)(2,1)}, bf16[6,170,8,64]{1,3,2,0:T(8,128)(2,1)}, u32[]{:S(2)}, u32[]{:S(2)}) collective-permute-start(bf16[6,170,8,64]{1,3,2,0:T(8,128)(2,1)} %multiply_convert_fusion.3), channel_id=1, source_target_pairs={{0,4},{2,6},{4,0},{6,2},{1,5},{3,7},{5,1},{7,3},{8,12},{10,14},{12... | collective-permute-start | bytes 3133448 | tf_op jit(solution)/shard_map/ppermute | solution.py:42
  112.6 129.0 %collective-permute-start.3 = (bf16[6,170,8,64]{1,3,2,0:T(8,128)(2,1)}, bf16[6,170,8,64]{1,3,2,0:T(8,128)(2,1)}, u32[]{:S(2)}, u32[]{:S(2)}) collective-permute-start(bf16[6,170,8,64]{1,3,2,0:T(8,128)(2,1)} %multiply_convert_fusion.3), channel_id=1, source_target_pairs={{0,2},{2,4},{4,6},{6,0},{1,3},{3,5},{5,7},{7,1},{8,10},{10,12},{12... | collective-permute-start | bytes 3133448 | tf_op jit(solution)/shard_map/ppermute | solution.py:42
  121.0 120.6 %copy-start.30 = (f32[6,170,8]{1,2,0:T(8,128)}, f32[6,170,8]{1,2,0:T(8,128)S(1)}, u32[]{:S(2)}) copy-start(f32[6,170,8]{1,2,0:T(8,128)S(1)} %add_rsqrt_fusion.1) | copy-start | bytes 97924
  173.7 100.0 %collective-permute-start = (bf16[6,170,8,64]{1,3,2,0:T(8,128)(2,1)}, bf16[6,170,8,64]{1,3,2,0:T(8,128)(2,1)}, u32[]{:S(2)}, u32[]{:S(2)}) collective-permute-start(bf16[6,170,8,64]{1,3,2,0:T(8,128)(2,1)} %add_convert_fusion.2), channel_id=1, source_target_pairs={{0,2},{2,4},{4,6},{6,0},{1,3},{3,5},{5,7},{7,1},{8,10},{10,12},{12... | collective-permute-start | bytes 3133448 | tf_op jit(solution)/shard_map/ppermute | solution.py:42
  241.7 17.0 %copy-start.11 = (pred[6,170,4,170]{1,3,2,0:T(8,128)(4,1)S(1)}, pred[6,170,4,170]{1,3,2,0:T(8,128)(4,1)}, u32[]{:S(2)}) copy-start(pred[6,170,4,170]{1,3,2,0:T(8,128)(4,1)} %broadcast_compare_fusion) | copy-start | bytes 2080804
  258.6 15.0 %copy-start.17 = (bf16[1,6,170,8,64]{2,4,0,3,1:T(8,128)(2,1)S(1)}, bf16[1,6,170,8,64]{2,4,0,3,1:T(8,128)(2,1)}, u32[]{:S(2)}) copy-start(bf16[1,6,170,8,64]{2,4,0,3,1:T(8,128)(2,1)} %add_convert_fusion.3) | copy-start | bytes 3133444
  311.4 12.3 %collective-permute-start.6 = (f32[1020,1024]{1,0:T(8,128)}, f32[1020,1024]{1,0:T(8,128)}, u32[]{:S(2)}, u32[]{:S(2)}) collective-permute-start(f32[1020,1024]{1,0:T(8,128)} %fusion.85), channel_id=1, source_target_pairs={{0,1},{1,0},{2,3},{3,2},{4,5},{5,4},{6,7},{7,6},{8,9},{9,8},{10,11... | collective-permute-start | bytes 12533768 | tf_op jit(solution)/shard_map/ppermute | solution.py:34
  311.4 533.6 %reduce-scatter.9.cloned.1.call-start = ((), (), s32[]{:S(2)}) async-start(), calls=%async_computation.10 | async-start | bytes 1310720 | tf_op jit(solution)/shard_map/reduce_scatter | solution.py:238
  346.3 46.4 %copy-start.18 = (bf16[1020,1024]{1,0:T(8,128)(2,1)S(1)}, bf16[1020,1024]{1,0:T(8,128)(2,1)}, u32[]{:S(2)}) copy-start(bf16[1020,1024]{1,0:T(8,128)(2,1)} %reshape.315) | copy-start | bytes 6266884
  346.3 46.4 %copy-start.58 = (f32[2048]{0:T(1024)S(1)}, f32[2048]{0:T(1024)}, u32[]{:S(2)}) copy-start(f32[2048]{0:T(1024)} %param.28) | copy-start | bytes 24580
  413.1 15.2 %collective-permute-start.8 = (f32[1020,1024]{1,0:T(8,128)}, f32[1020,1024]{1,0:T(8,128)}, u32[]{:S(2)}, u32[]{:S(2)}) collective-permute-start(f32[1020,1024]{1,0:T(8,128)} %fusion.45), channel_id=1, source_target_pairs={{0,1},{1,0},{2,3},{3,2},{4,5},{5,4},{6,7},{7,6},{8,9},{9,8},{10,11... | collective-permute-start | bytes 12533768 | tf_op jit(solution)/shard_map/ppermute | solution.py:34
  421.6 17.7 %collective-permute-start.7 = (f32[1020,1024]{1,0:T(8,128)}, f32[1020,1024]{1,0:T(8,128)}, u32[]{:S(2)}, u32[]{:S(2)}) collective-permute-start(f32[1020,1024]{1,0:T(8,128)} %fusion.74), channel_id=1, source_target_pairs={{0,1},{1,0},{2,3},{3,2},{4,5},{5,4},{6,7},{7,6},{8,9},{9,8},{10,11... | collective-permute-start | bytes 12533768 | tf_op jit(solution)/shard_map/ppermute | solution.py:34
  480.1 364.9 %reduce-scatter.11.cloned.1.call-start = ((), (), s32[]{:S(2)}) async-start(), calls=%async_computation.11 | async-start | bytes 5242880 | tf_op jit(solution)/shard_map/reduce_scatter | solution.py:237
  488.5 356.5 %reduce-scatter.13.cloned.1.call-start = ((), (), s32[]{:S(2)}) async-start(), calls=%async_computation.12 | async-start | bytes 5242880 | tf_op jit(solution)/shard_map/reduce_scatter | solution.py:239
  504.6 340.4 %reduce-scatter.7.cloned.1.call-start = ((), (), s32[]{:S(2)}) async-start(), calls=%async_computation.9 | async-start | bytes 3932160 | tf_op jit(solution)/shard_map/reduce_scatter | solution.py:236
  567.1 52.0 %collective-permute-start.12 = (bf16[6,170,8,64]{1,3,2,0:T(8,128)(2,1)}, bf16[6,170,8,64]{1,3,2,0:T(8,128)(2,1)}, u32[]{:S(2)}, u32[]{:S(2)}) collective-permute-start(bf16[6,170,8,64]{1,3,2,0:T(8,128)(2,1)} %get-tuple-element.119), channel_id=1, source_target_pairs={{0,6},{2,0},{4,2},{6,4},{1,7},{3,1},{5,3},{7,5},{8,14},{10,8},{12,... | collective-permute-start | bytes 3133448 | tf_op jit(solution)/shard_map/ppermute | solution.py:51
  569.5 69.9 %collective-permute-start.14 = (bf16[6,170,8,64]{1,3,2,0:T(8,128)(2,1)}, bf16[6,170,8,64]{1,3,2,0:T(8,128)(2,1)}, u32[]{:S(2)}, u32[]{:S(2)}) collective-permute-start(bf16[6,170,8,64]{1,3,2,0:T(8,128)(2,1)} %get-tuple-element.120), channel_id=1, source_target_pairs={{0,2},{2,4},{4,6},{6,0},{1,3},{3,5},{5,7},{7,1},{8,10},{10,12},{12... | collective-permute-start | bytes 3133448 | tf_op jit(solution)/shard_map/ppermute | solution.py:51
  569.5 71.3 %collective-permute-start.13 = (bf16[6,170,8,64]{1,3,2,0:T(8,128)(2,1)}, bf16[6,170,8,64]{1,3,2,0:T(8,128)(2,1)}, u32[]{:S(2)}, u32[]{:S(2)}) collective-permute-start(bf16[6,170,8,64]{1,3,2,0:T(8,128)(2,1)} %get-tuple-element.121), channel_id=1, source_target_pairs={{0,4},{2,6},{4,0},{6,2},{1,5},{3,7},{5,1},{7,3},{8,12},{10,14},{12... | collective-permute-start | bytes 3133448 | tf_op jit(solution)/shard_map/ppermute | solution.py:51
  570.7 29.9 %copy-start.7 = (f32[6,170,1,512]{1,3,0,2:T(8,128)S(1)}, f32[6,170,1,512]{1,3,0,2:T(8,128)}, u32[]{:S(2)}) copy-start(f32[6,170,1,512]{1,3,0,2:T(8,128)} %copy.127) | copy-start | bytes 6266884
  570.7 29.9 %copy-start.31 = (f32[6,170,8]{1,2,0:T(8,128)S(1)}, f32[6,170,8]{1,2,0:T(8,128)}, u32[]{:S(2)}) copy-start(f32[6,170,8]{1,2,0:T(8,128)} %copy-done.30) | copy-start | bytes 97924
  570.7 30.0 %copy-start.44 = (f32[8,64]{1,0:T(8,128)S(1)}, f32[8,64]{1,0:T(8,128)}, u32[]{:S(2)}) copy-start(f32[8,64]{1,0:T(8,128)} %copy-done.43) | copy-start | bytes 6148
  570.7 30.0 %copy-start.52 = (f32[8]{0:T(128)S(1)}, f32[8]{0:T(128)}, u32[]{:S(2)}) copy-start(f32[8]{0:T(128)} %copy-done.51) | copy-start | bytes 100
  616.7 55.5 %collective-permute-start.9 = (bf16[6,170,8,64]{1,3,2,0:T(8,128)(2,1)}, bf16[6,170,8,64]{1,3,2,0:T(8,128)(2,1)}, u32[]{:S(2)}, u32[]{:S(2)}) collective-permute-start(bf16[6,170,8,64]{1,3,2,0:T(8,128)(2,1)} %get-tuple-element.116), channel_id=1, source_target_pairs={{0,6},{2,0},{4,2},{6,4},{1,7},{3,1},{5,3},{7,5},{8,14},{10,8},{12,... | collective-permute-start | bytes 3133448 | tf_op jit(solution)/shard_map/ppermute | solution.py:51
  618.9 87.6 %collective-permute-start.11 = (bf16[6,170,8,64]{1,3,2,0:T(8,128)(2,1)}, bf16[6,170,8,64]{1,3,2,0:T(8,128)(2,1)}, u32[]{:S(2)}, u32[]{:S(2)}) collective-permute-start(bf16[6,170,8,64]{1,3,2,0:T(8,128)(2,1)} %get-tuple-element.117), channel_id=1, source_target_pairs={{0,2},{2,4},{4,6},{6,0},{1,3},{3,5},{5,7},{7,1},{8,10},{10,12},{12... | collective-permute-start | bytes 3133448 | tf_op jit(solution)/shard_map/ppermute | solution.py:51
  619.1 88.4 %collective-permute-start.10 = (bf16[6,170,8,64]{1,3,2,0:T(8,128)(2,1)}, bf16[6,170,8,64]{1,3,2,0:T(8,128)(2,1)}, u32[]{:S(2)}, u32[]{:S(2)}) collective-permute-start(bf16[6,170,8,64]{1,3,2,0:T(8,128)(2,1)} %get-tuple-element.118), channel_id=1, source_target_pairs={{0,4},{2,6},{4,0},{6,2},{1,5},{3,7},{5,1},{7,3},{8,12},{10,14},{12... | collective-permute-start | bytes 3133448 | tf_op jit(solution)/shard_map/ppermute | solution.py:51
  645.8 61.8 %copy-start.2 = (f32[6,170,1,512]{1,3,0,2:T(8,128)S(1)}, f32[6,170,1,512]{1,3,0,2:T(8,128)}, u32[]{:S(2)}) copy-start(f32[6,170,1,512]{1,3,0,2:T(8,128)} %copy-done.1) | copy-start | bytes 6266884
  658.5 53.4 %copy-start.27 = (f32[6,170,8]{1,2,0:T(8,128)S(1)}, f32[6,170,8]{1,2,0:T(8,128)}, u32[]{:S(2)}) copy-start(f32[6,170,8]{1,2,0:T(8,128)} %copy-done.26) | copy-start | bytes 97924
  658.5 53.5 %copy-start.25 = (f32[6,170,8]{1,2,0:T(8,128)S(1)}, f32[6,170,8]{1,2,0:T(8,128)}, u32[]{:S(2)}) copy-start(f32[6,170,8]{1,2,0:T(8,128)} %copy-done.24) | copy-start | bytes 97924
  745.9 185.4 %all-reduce.6.cloned.1.call-start = ((), (), s32[]{:S(2)}) async-start(), calls=%async_computation.13 | async-start | bytes 6291456 | tf_op jit(solution)/shard_map/psum | solution.py:241
  752.9 81.1 %collective-permute-start.15 = (f32[1020,1024]{1,0:T(8,128)}, f32[1020,1024]{1,0:T(8,128)}, u32[]{:S(2)}, u32[]{:S(2)}) collective-permute-start(f32[1020,1024]{1,0:T(8,128)} %fusion.87), channel_id=1, source_target_pairs={{0,1},{1,0},{2,3},{3,2},{4,5},{5,4},{6,7},{7,6},{8,9},{9,8},{10,11... | collective-permute-start | bytes 12533768 | tf_op jit(solution)/shard_map/ppermute | solution.py:34
  890.0 20.6 %all-to-all-start = ((f32[4,6,256]{2,1,0:T(8,128)}), f32[4,6,256]{2,1,0:T(8,128)S(1)}, u32[]{:S(2)}, u32[]{:S(2)}) async-start(f32[4,6,256]{2,1,0:T(8,128)} %fusion.88), calls=%async_computation | async-start | bytes 65536 | tf_op jit(solution)/shard_map/all_to_all | solution.py:232
  (44 other events, 267.5 us)
Sparse Core Ops, SparseCore 0:
  10.1 79.1 all-gather.6
  90.9 31.7 all-gather.8
  124.3 79.0 all-gather.10
  311.5 81.1 all-gather.12
  480.3 25.5 reduce-scatter.8
  508.1 75.3 reduce-scatter.10
  585.7 77.2 reduce-scatter.12
  746.0 58.2 reduce-scatter.6
  845.2 86.0 all-reduce.5
where the time goes:
time: 957 us; the launch traced here: 947 us
  waiting for transfers between devices  239 us (25%)
  matrix products  205 us (21%)
  other arithmetic  165 us (17%)
  blocking collectives  161 us (17%)
  local copies, waits for them, and re-layouts  137 us (14%)
  starting transfers between devices  24.2 us (3%)
  between operations  15.9 us (2%)
    ppermute x6, waiting for transfers between devices, ctx_shifts(): parts.append(lax.ppermute(values, 'ctx', pairs))  115 us
    psum x1, blocking collectives, body(): small_flat = lax.psum(jnp.concatenate(small_parts), ('shard', 'ctx'))  75.6 us
    ppermute x6, waiting for transfers between devices, ctx_return(): total = total + lax.ppermute(parts[shift], 'ctx', pairs).astype(jnp.float32)  59.5 us
    unnamed x1, blocking collectives  36 us
    all_gather x1, waiting for transfers between devices, body(): lax.all_gather(down_weight, 'shard', axis=1, tiled=True)  35.6 us
    convert_element_type x1, other arithmetic, body(): d_scores = (probs * (d_probs - row_delta)).astype(jnp.bfloat16)  29.9 us
    dot_general x1, matrix products, body(): jnp.einsum('mqhd,nmkhd->mhqnk', d_heads, values_parts, preferred_element_...  29 us
    unnamed x147, local copies, waits for them, and re-layouts  27.6 us
  transfers between devices with their start and end apart: 27, of which 11 were waited for; matrix products, arithmetic and copies ran while one was open for 49% of the time, Pallas kernels for 0%

commit v1 on v0

--- a/solution.py
+++ b/solution.py
@@ -238,7 +238,9 @@
         lax.psum_scatter(g_proj.astype(jnp.bfloat16), "shard", scatter_dimension=1, tiled=True),
         lax.psum_scatter(g_down.astype(jnp.bfloat16), "shard", scatter_dimension=1, tiled=True),
     )
-    summed = tuple((lax.psum(g, "ctx").astype(jnp.float32) for g in shard_grads))
+    summed = tuple(
+        (jnp.sum(lax.all_gather(g, "ctx"), axis=0).astype(jnp.float32) for g in shard_grads)
+    )
     square_sums = jnp.stack(
         [jnp.sum(stream * stream), jnp.sum(attn_part * attn_part), jnp.sum(mlp_part * mlp_part)]
     )

time: 957 us -> 1010 us (1.055)
  waiting for transfers between devices: 239 us -> 281 us
    reduce_scatter x1, waiting for transfers between devices: 0.01 us -> 48.3 us  [body(): lax.psum_scatter(g_qkv.astype(jnp.bfloat16), 'shard', scatter_dimension=0...]
    psum x1 -> x0, waiting for transfers between devices: 20.1 us -> none  [body(): lax.psum(g, 'ctx').astype(jnp.float32)]
    all_gather x0 -> x4, waiting for transfers between devices: none -> 12.7 us  [body(): lax.all_gather(g, 'ctx')]
    reduce_sum x0 -> x4, other arithmetic: none -> 10.9 us  [body(): jnp.sum(lax.all_gather(g, 'ctx'), axis=0).astype(jnp.float32)]
    unnamed x147 -> x145, local copies, waits for them, and re-layouts: 27.6 us -> 27.6 us
  transfers between devices with their start and end apart: 27 -> 30, of which waited for: 11 -> 12; matrix products, arithmetic and copies ran while one was open for 49% -> 48% of each run, Pallas kernels for 0% -> 0%
where the time goes in v1:
time: 1010 us; the launch traced here: 1000 us
  waiting for transfers between devices  281 us (28%)
  matrix products  205 us (20%)
  other arithmetic  172 us (17%)
  blocking collectives  163 us (16%)
  local copies, waits for them, and re-layouts  137 us (14%)
  starting transfers between devices  24.3 us (2%)
  between operations  16.3 us (2%)
    ppermute x6, waiting for transfers between devices, ctx_shifts(): parts.append(lax.ppermute(values, 'ctx', pairs))  115 us
    psum x1, blocking collectives, body(): small_flat = lax.psum(jnp.concatenate(small_parts), ('shard', 'ctx'))  76.7 us
    ppermute x6, waiting for transfers between devices, ctx_return(): total = total + lax.ppermute(parts[shift], 'ctx', pairs).astype(jnp.float32)  59.4 us
    reduce_scatter x1, waiting for transfers between devices, body(): lax.psum_scatter(g_qkv.astype(jnp.bfloat16), 'shard', scatter_dimension=0...  48.3 us
    unnamed x1, blocking collectives  36 us
    all_gather x1, waiting for transfers between devices, body(): lax.all_gather(down_weight, 'shard', axis=1, tiled=True)  35.6 us
    convert_element_type x1, other arithmetic, body(): d_scores = (probs * (d_probs - row_delta)).astype(jnp.bfloat16)  30 us
    dot_general x1, matrix products, body(): jnp.einsum('mqhd,nmkhd->mhqnk', d_heads, values_parts, preferred_element_...  28.9 us
  transfers between devices with their start and end apart: 30, of which 12 were waited for; matrix products, arithmetic and copies ran while one was open for 48% of the time, Pallas kernels for 0%

profile of v1, /device:TPU:0, one launch (start us, length us, event | category | flops | bytes accessed | tf_op | source)
XLA Modules:
  0.0 1000.0 jit_solution(12573023106836706265)
XLA Ops:
  10.3 15.2 %all-gather.4 = bf16[4,6,1024]{2,1,0:T(8,128)(2,1)S(1)} all-gather(bf16[1,6,1024]{2,1,0:T(8,128)(2,1)} %bitcast.230), channel_id=1, replica_groups=mesh['shard'=4,'ctx'=4,'tp'=2] {'shard'}, dimensions={0}, use_global_device_ids=true | all-gather | bytes 61440 | tf_op jit(solution)/shard_map/all_gather | solution.py:94
  33.3 36.0 %fusion = f32[8,6144]{1,0:T(8,128)S(1)} fusion(f32[24,6144]{1,0:T(8,128)S(1)} %fusion.72), kind=kCustom, calls=%all-reduce-scatter | all-reduce-scatter fusion | flops 196609 | bytes 786944
  84.2 5.2 all-gather.15.cloned.1.call-done
  89.3 6.1 fusion.39
  124.1 49.5 %collective-permute-done.5 = bf16[6,170,8,64]{1,3,2,0:T(8,128)(2,1)} collective-permute-done((bf16[6,170,8,64]{1,3,2,0:T(8,128)(2,1)}, bf16[6,170,8,64]{1,3,2,0:T(8,128)(2,1)}, u32[]{:S(2)}, u32[]{:S(2)}) %collective-permute-start.5) | collective-permute-done | bytes 1044512 | tf_op jit(solution)/shard_map/ppermute | solution.py:42
  176.1 65.5 %collective-permute-done.4 = bf16[6,170,8,64]{1,3,2,0:T(8,128)(2,1)} collective-permute-done((bf16[6,170,8,64]{1,3,2,0:T(8,128)(2,1)}, bf16[6,170,8,64]{1,3,2,0:T(8,128)(2,1)}, u32[]{:S(2)}, u32[]{:S(2)}) %collective-permute-start.4) | collective-permute-done | bytes 1044512 | tf_op jit(solution)/shard_map/ppermute | solution.py:42
  241.7 17.0 %select_reduce_fusion = (f32[6,8,170]{2,1,0:T(8,128)S(1)}, f32[6,8,170,4,170]{2,4,3,1,0:T(8,128)}) fusion(pred[6,170,4,170]{1,3,2,0:T(8,128)(4,1)} %broadcast_compare_fusion, bf16[1,6,170,8,64]{2,4,0,3,1:T(8,128)(2,1)} %bitcast.26, bf16[1,6,170,8,64]{2,4,0,3,1:T(8,128)(2,1)} %bitcast.25, bf16[1,6,170,8,64]{2,4,0,3,1:T(8,128)(2,1)} %bitcast.23, ...), kind=kOutput, calls=%fused_computation.6 | convolution fusion | flops 740136448 | bytes 29223040 | tf_op jit(solution)/shard_map/mqhd,nmkhd->mhqnk/dot_general | solution.py:135
  258.6 14.9 %fusion.1 = f32[6,8,170]{2,1,0:T(8,128)S(1)} fusion(f32[6,8,170,4,170]{2,4,3,1,0:T(8,128)} %get-tuple-element.129, f32[6,8,170]{2,1,0:T(8,128)S(1)} %get-tuple-element.128, pred[6,170,4,170]{1,3,2,0:T(8,128)(4,1)S(1)} %copy-done.11), kind=kLoop, calls=%fused_computation.5 | loop fusion | flops 16638240 | bytes 22954080 | tf_op jit(solution)/shard_map/reduce_sum | solution.py:143
  273.6 18.0 %fusion.51 = bf16[6,170,8,64]{1,3,2,0:T(8,128)(2,1)} fusion(f32[6,8,170,4,170]{2,4,3,1,0:T(8,128)} %get-tuple-element.129, f32[6,8,170]{2,1,0:T(8,128)S(1)} %fusion.1, f32[6,8,170]{2,1,0:T(8,128)S(1)} %get-tuple-element.128, pred[6,170,4,170]{1,3,2,0:T(8,128)(4,1)S(1)} %copy-done.11, bf16[1,6,170,8,64]{2,4,0,3,1:T(8,128)(2,1)} %bitcast.15, ...), kind=kOutput, calls=%fused_computation.109 | convolution fusion | flops 739230720 | bytes 28176480 | tf_op jit(solution)/shard_map/mhqnk,nmkhd->mqhd/dot_general | solution.py:146
  291.7 12.4 %copy.134 = bf16[6,170,8,64]{3,2,1,0:T(8,128)(2,1)S(1)} copy(bf16[6,170,8,64]{1,3,2,0:T(8,128)(2,1)} %fusion.51) | data formatting | bytes 2088960 | tf_op jit(solution)/shard_map/convert_element_type | solution.py:149
  306.4 5.0 fusion.85
  323.7 9.4 multiply_reduce_fusion.7
  346.3 10.8 %fusion.86 = f32[1020,2048]{1,0:T(8,128)} fusion(bf16[1020,1024]{1,0:T(8,128)(2,1)} %reshape.313, bf16[1024,2048]{1,0:T(8,128)(2,1)} %all-gather.19.cloned.1.call-done), kind=kOutput, calls=%fused_computation.178 | convolution fusion | flops 4278190080 | bytes 14639104 | tf_op jit(solution)/shard_map/dot_general | solution.py:156
  357.1 35.6 %all-gather.21.cloned.1.call-done = bf16[2048,1024]{1,0:T(8,128)(2,1)} async-done(((bf16[2048,256]{1,0:T(8,128)(2,1)}), bf16[2048,1024]{1,0:T(8,128)(2,1)}) %all-gather.21.cloned.1.call-update) | async-done | bytes 4194320 | tf_op jit(solution)/shard_map/all_gather | solution.py:90
  392.7 14.2 %fusion.76 = (f32[2048]{0:T(1024)}, bf16[1020,2048]{1,0:T(8,128)(2,1)S(1)}) fusion(f32[1020,2048]{1,0:T(8,128)} %fusion.86, f32[2048]{0:T(1024)S(1)} %copy-done.57, bf16[1020,1024]{1,0:T(8,128)(2,1)S(1)} %copy-done.18, bf16[2048,1024]{1,0:T(8,128)(2,1)} %all-gather.21.cloned.1.call-done), kind=kOutput, calls=%fused_computation.170 | convolution fusion | flops 4324145152 | bytes 18833408 | tf_op jit(solution)/shard_map/rd,fd->rf/dot_general | solution.py:169
  406.9 6.2 fusion.45
  414.5 7.0 fusion.74
  428.3 6.9 add.307
  439.3 9.3 multiply_reduce_fusion.6
  452.9 8.9 multiply_reduce_fusion.1
  466.1 5.2 multiply_reduce_fusion.8
  480.2 8.3 convolution_convert_fusion.1
  492.0 12.7 %convolution_convert_fusion = bf16[2048,1024]{1,0:T(8,128)(2,1)} fusion(bf16[1020,1024]{1,0:T(8,128)(2,1)} %reshape.315, f32[1020,2048]{1,0:T(8,128)} %fusion.86, f32[2048]{0:T(1024)S(1)} %copy-done.57), kind=kOutput, calls=%fused_computation.65 | convolution fusion | flops 4301176832 | bytes 14647296 | tf_op jit(solution)/shard_map/rf,rd->fd/dot_general | solution.py:168
  516.6 16.9 %convert_bitcast_fusion = bf16[4,6,170,8,64]{2,4,0,3,1:T(8,128)(2,1)} fusion(bf16[6,170,8,64,1]{1,3,4,2,0:T(8,128)(2,1)S(1)} %copy.156, f32[6,8,170,4,170]{2,4,3,1,0:T(8,128)} %get-tuple-element.129, f32[6,8,170]{2,1,0:T(8,128)S(1)} %log_add_fusion, pred[6,170,4,170]{1,3,2,0:T(8,128)(4,1)S(1)} %copy-done.11), kind=kOutput, calls=%fused_computation.39 | convolution fusion | flops 728981760 | bytes 28143840 | tf_op jit(solution)/shard_map/mhqnk,mqhd->nmkhd/dot_general | solution.py:198
  533.4 28.9 %multiply_reduce_fusion = (f32[6,8,170]{2,1,0:T(8,128)S(1)}, f32[6,8,170,4,170]{2,4,3,1,0:T(8,128)}) fusion(f32[6,8,170,4,170]{2,4,3,1,0:T(8,128)} %get-tuple-element.129, f32[6,8,170]{2,1,0:T(8,128)S(1)} %log_add_fusion, pred[6,170,4,170]{1,3,2,0:T(8,128)(4,1)S(1)} %copy-done.11, bf16[6,170,8,64,1]{1,3,4,2,0:T(8,128)(2,1)S(1)} %copy.156, ...), kind=kOutput, calls=%fused_computation.1 | convolution fusion | flops 749145088 | bytes 50371680 | tf_op jit(solution)/shard_map/mqhd,nmkhd->mhqnk/dot_general | solution.py:186
  570.7 30.0 %multiply_convert_fusion = bf16[6,8,170,4,170]{2,4,3,1,0:T(8,128)(2,1)} fusion(f32[6,8,170,4,170]{2,4,3,1,0:T(8,128)} %get-tuple-element.131, f32[6,8,170,4,170]{2,4,3,1,0:T(8,128)} %get-tuple-element.129, f32[6,8,170]{2,1,0:T(8,128)S(1)} %get-tuple-element.130, f32[6,8,170]{2,1,0:T(8,128)S(1)} %log_add_fusion, pred[6,170,4,170]{1,3,2,0:T(8,128)(4,1)} %broadcast_compare_fusion), kind=kLoop, calls=%fused_computation | loop fusion | flops 27744000 | bytes 56246880 | tf_op jit(solution)/shard_map/convert_element_type | solution.py:190
  600.7 11.2 %convert_bitcast_fusion.1 = bf16[4,6,170,8,64]{2,4,3,1,0:T(8,128)(2,1)} fusion(bf16[6,8,170,4,170]{2,4,3,1,0:T(8,128)(2,1)} %multiply_convert_fusion, f32[6,170,8,64]{1,3,2,0:T(8,128)S(1)} %bitcast.191, f32[8]{0:T(128)S(1)} %copy-done.51, f32[6,170,8]{1,2,0:T(8,128)S(1)} %copy-done.30, f32[8,64]{1,0:T(8,128)S(1)} %copy-done.43), kind=kOutput, calls=%fused_computation.40 | convolution fusion | flops 714424320 | bytes 17399200 | tf_op jit(solution)/shard_map/mhqnk,mqhd->nmkhd/dot_general | solution.py:195
  611.9 4.8 slice_bitcast_fusion.6
  620.8 9.6 fusion.41
  630.4 9.0 collective-permute-done.14
  640.8 5.0 fusion.78
  645.8 6.4 copy.146
  652.2 6.3 copy.144
  658.5 13.7 %collective-permute-done.9 = bf16[6,170,8,64]{1,3,2,0:T(8,128)(2,1)} collective-permute-done((bf16[6,170,8,64]{1,3,2,0:T(8,128)(2,1)}, bf16[6,170,8,64]{1,3,2,0:T(8,128)(2,1)}, u32[]{:S(2)}, u32[]{:S(2)}) %collective-permute-start.9) | collective-permute-done | bytes 1044512 | tf_op jit(solution)/shard_map/ppermute | solution.py:51
  672.1 34.3 %collective-permute-done.11 = bf16[6,170,8,64]{1,3,2,0:T(8,128)(2,1)} collective-permute-done((bf16[6,170,8,64]{1,3,2,0:T(8,128)(2,1)}, bf16[6,170,8,64]{1,3,2,0:T(8,128)(2,1)}, u32[]{:S(2)}, u32[]{:S(2)}) %collective-permute-start.11) | collective-permute-done | bytes 1044512 | tf_op jit(solution)/shard_map/ppermute | solution.py:51
  711.9 5.7 add_add_fusion.2
  717.6 6.4 copy.145
  724.1 8.3 maximum_convert_fusion
  738.2 7.7 convolution_convert_fusion.2
  748.1 7.4 fusion.87
  755.5 48.3 %reduce-scatter.7.cloned.1.call-done = bf16[256,3,512]{2,0,1:T(8,128)(2,1)} async-done(((bf16[1024,3,512]{2,0,1:T(8,128)(2,1)}), bf16[256,3,512]{2,0,1:T(8,128)(2,1)}) %reduce-scatter.7.cloned.1.call-update) | async-done | bytes 786448 | tf_op jit(solution)/shard_map/reduce_scatter | solution.py:236
  806.1 76.7 %psum.15 = f32[5131]{0:T(1024)S(1)} all-reduce(f32[5131]{0:T(1024)S(1)} %concatenate.3), channel_id=1, replica_groups=mesh['shard'=4,'ctx'=4,'tp'=2] {'shard','ctx'}, use_global_device_ids=true, to_apply=%region_37.38 | all-reduce | flops 5131 | bytes 41048 | tf_op jit(solution)/shard_map/psum | solution.py:256
  888.2 6.9 add.315
  905.7 21.2 %all-reduce.3 = bf16[6,6,1024]{2,1,0:T(8,128)(2,1)S(1)} all-reduce(f32[6,6,1024]{2,1,0:T(8,128)S(1)} %stack.61), channel_id=1, replica_groups=mesh['shard'=4,'ctx'=4,'tp'=2] {'ctx'}, use_global_device_ids=true, to_apply=%region_24.25 | all-reduce | flops 36864 | bytes 221184 | tf_op jit(solution)/shard_map/psum | solution.py:225
  927.1 14.3 %all-gather.5 = bf16[4,6,6144]{2,1,0:T(8,128)(2,1)S(1)} all-gather(bf16[1,6,6144]{2,1,0:T(8,128)(2,1)S(1)} %reshape.336), channel_id=1, replica_groups=mesh['shard'=4,'ctx'=4,'tp'=2] {'shard'}, dimensions={0}, use_global_device_ids=true | all-gather | bytes 368640 | tf_op jit(solution)/shard_map/all_gather | solution.py:226
  952.6 5.6 add_convert_fusion
  958.9 6.6 copy.151
  976.1 12.7 %all-gather.23.cloned.1.call-done = bf16[1024,3,512]{2,0,1:T(8,128)(2,1)} async-done(((bf16[256,3,512]{2,0,1:T(8,128)(2,1)}), bf16[1024,3,512]{2,0,1:T(8,128)(2,1)}) %all-gather.23.cloned.1.call-update) | async-done | bytes 3145744 | tf_op jit(solution)/shard_map/all_gather | solution.py:242
  (306 shorter events, 200.5 us)
Async XLA Ops:
  7.2 82.1 %all-gather.15.cloned.1.call-start = ((), (), s32[]{:S(2)}) async-start(), calls=%async_computation.5 | async-start | bytes 3932160 | tf_op jit(solution)/shard_map/all_gather | solution.py:87
  9.5 296.8 %all-gather.17.cloned.1.call-start = ((), (), s32[]{:S(2)}) async-start(), calls=%async_computation.6 | async-start | bytes 1310720 | tf_op jit(solution)/shard_map/all_gather | solution.py:89
  10.3 336.0 %all-gather.19.cloned.1.call-start = ((), (), s32[]{:S(2)}) async-start(), calls=%async_computation.7 | async-start | bytes 5242880 | tf_op jit(solution)/shard_map/all_gather | solution.py:88
  30.3 42.4 %copy-start.52 = (f32[512]{0:T(512)S(1)}, f32[512]{0:T(512)}, u32[]{:S(2)}) copy-start(f32[512]{0:T(512)} %param.22) | copy-start | bytes 6148
  30.3 42.5 %copy-start.53 = (f32[512]{0:T(512)S(1)}, f32[512]{0:T(512)}, u32[]{:S(2)}) copy-start(f32[512]{0:T(512)} %param.23) | copy-start | bytes 6148
  30.3 42.6 %copy-start.49 = (s32[6,10]{1,0:T(8,128)S(1)}, s32[6,10]{1,0:T(8,128)}, u32[]{:S(2)}) copy-start(s32[6,10]{1,0:T(8,128)} %param.18) | copy-start | bytes 724
  30.3 42.8 %copy-start.3 = (bf16[6,170,1024]{2,1,0:T(8,128)(2,1)S(1)}, bf16[6,170,1024]{2,1,0:T(8,128)(2,1)}, u32[]{:S(2)}) copy-start(bf16[6,170,1024]{2,1,0:T(8,128)(2,1)} %param.16) | copy-start | bytes 6266884
  69.3 10.3 %collective-permute-start.16 = (f32[6,6144]{1,0:T(8,128)S(1)}, f32[6,6144]{1,0:T(8,128)S(1)}, u32[]{:S(2)}, u32[]{:S(2)}) collective-permute-start(f32[6,6144]{1,0:T(8,128)S(1)} %slice.120), channel_id=1, source_target_pairs={{0,8},{8,16},{16,24},{1,9},{9,17},{17,25},{2,10},{10,18},{18,26},{... | collective-permute-start | bytes 442376
  72.5 320.2 %all-gather.21.cloned.1.call-start = ((), (), s32[]{:S(2)}) async-start(), calls=%async_computation.8 | async-start | bytes 5242880 | tf_op jit(solution)/shard_map/all_gather | solution.py:90
  72.6 169.1 %copy-start.50 = (f32[8]{0:T(128)}, f32[8]{0:T(128)S(1)}, u32[]{:S(2)}) copy-start(f32[8]{0:T(128)S(1)} %exp.18) | copy-start | bytes 100
  72.7 168.9 %copy-start.42 = (f32[8,64]{1,0:T(8,128)}, f32[8,64]{1,0:T(8,128)S(1)}, u32[]{:S(2)}) copy-start(f32[8,64]{1,0:T(8,128)S(1)} %add.284) | copy-start | bytes 6148
  102.3 171.3 %collective-permute-start.2 = (bf16[6,170,8,64]{1,3,2,0:T(8,128)(2,1)}, bf16[6,170,8,64]{1,3,2,0:T(8,128)(2,1)}, u32[]{:S(2)}, u32[]{:S(2)}) collective-permute-start(bf16[6,170,8,64]{1,3,2,0:T(8,128)(2,1)} %add_convert_fusion.2), channel_id=1, source_target_pairs={{0,6},{2,0},{4,2},{6,4},{1,7},{3,1},{5,3},{7,5},{8,14},{10,8},{12,... | collective-permute-start | bytes 3133448 | tf_op jit(solution)/shard_map/ppermute | solution.py:42
  104.8 168.8 %collective-permute-start.1 = (bf16[6,170,8,64]{1,3,2,0:T(8,128)(2,1)}, bf16[6,170,8,64]{1,3,2,0:T(8,128)(2,1)}, u32[]{:S(2)}, u32[]{:S(2)}) collective-permute-start(bf16[6,170,8,64]{1,3,2,0:T(8,128)(2,1)} %add_convert_fusion.2), channel_id=1, source_target_pairs={{0,4},{2,6},{4,0},{6,2},{1,5},{3,7},{5,1},{7,3},{8,12},{10,14},{12... | collective-permute-start | bytes 3133448 | tf_op jit(solution)/shard_map/ppermute | solution.py:42
  110.6 63.1 %collective-permute-start.5 = (bf16[6,170,8,64]{1,3,2,0:T(8,128)(2,1)}, bf16[6,170,8,64]{1,3,2,0:T(8,128)(2,1)}, u32[]{:S(2)}, u32[]{:S(2)}) collective-permute-start(bf16[6,170,8,64]{1,3,2,0:T(8,128)(2,1)} %multiply_convert_fusion.3), channel_id=1, source_target_pairs={{0,6},{2,0},{4,2},{6,4},{1,7},{3,1},{5,3},{7,5},{8,14},{10,8},{12,... | collective-permute-start | bytes 3133448 | tf_op jit(solution)/shard_map/ppermute | solution.py:42
  111.1 130.6 %collective-permute-start.4 = (bf16[6,170,8,64]{1,3,2,0:T(8,128)(2,1)}, bf16[6,170,8,64]{1,3,2,0:T(8,128)(2,1)}, u32[]{:S(2)}, u32[]{:S(2)}) collective-permute-start(bf16[6,170,8,64]{1,3,2,0:T(8,128)(2,1)} %multiply_convert_fusion.3), channel_id=1, source_target_pairs={{0,4},{2,6},{4,0},{6,2},{1,5},{3,7},{5,1},{7,3},{8,12},{10,14},{12... | collective-permute-start | bytes 3133448 | tf_op jit(solution)/shard_map/ppermute | solution.py:42
  112.6 129.0 %collective-permute-start.3 = (bf16[6,170,8,64]{1,3,2,0:T(8,128)(2,1)}, bf16[6,170,8,64]{1,3,2,0:T(8,128)(2,1)}, u32[]{:S(2)}, u32[]{:S(2)}) collective-permute-start(bf16[6,170,8,64]{1,3,2,0:T(8,128)(2,1)} %multiply_convert_fusion.3), channel_id=1, source_target_pairs={{0,2},{2,4},{4,6},{6,0},{1,3},{3,5},{5,7},{7,1},{8,10},{10,12},{12... | collective-permute-start | bytes 3133448 | tf_op jit(solution)/shard_map/ppermute | solution.py:42
  121.0 120.6 %copy-start.29 = (f32[6,170,8]{1,2,0:T(8,128)}, f32[6,170,8]{1,2,0:T(8,128)S(1)}, u32[]{:S(2)}) copy-start(f32[6,170,8]{1,2,0:T(8,128)S(1)} %add_rsqrt_fusion.1) | copy-start | bytes 97924
  173.7 100.0 %collective-permute-start = (bf16[6,170,8,64]{1,3,2,0:T(8,128)(2,1)}, bf16[6,170,8,64]{1,3,2,0:T(8,128)(2,1)}, u32[]{:S(2)}, u32[]{:S(2)}) collective-permute-start(bf16[6,170,8,64]{1,3,2,0:T(8,128)(2,1)} %add_convert_fusion.2), channel_id=1, source_target_pairs={{0,2},{2,4},{4,6},{6,0},{1,3},{3,5},{5,7},{7,1},{8,10},{10,12},{12... | collective-permute-start | bytes 3133448 | tf_op jit(solution)/shard_map/ppermute | solution.py:42
  311.4 12.3 %collective-permute-start.6 = (f32[1020,1024]{1,0:T(8,128)}, f32[1020,1024]{1,0:T(8,128)}, u32[]{:S(2)}, u32[]{:S(2)}) collective-permute-start(f32[1020,1024]{1,0:T(8,128)} %fusion.85), channel_id=1, source_target_pairs={{0,1},{1,0},{2,3},{3,2},{4,5},{5,4},{6,7},{7,6},{8,9},{9,8},{10,11... | collective-permute-start | bytes 12533768 | tf_op jit(solution)/shard_map/ppermute | solution.py:34
  311.4 434.6 %reduce-scatter.9.cloned.1.call-start = ((), (), s32[]{:S(2)}) async-start(), calls=%async_computation.10 | async-start | bytes 1310720 | tf_op jit(solution)/shard_map/reduce_scatter | solution.py:238
  346.3 46.4 %copy-start.18 = (bf16[1020,1024]{1,0:T(8,128)(2,1)S(1)}, bf16[1020,1024]{1,0:T(8,128)(2,1)}, u32[]{:S(2)}) copy-start(bf16[1020,1024]{1,0:T(8,128)(2,1)} %reshape.315) | copy-start | bytes 6266884
  346.3 46.4 %copy-start.57 = (f32[2048]{0:T(1024)S(1)}, f32[2048]{0:T(1024)}, u32[]{:S(2)}) copy-start(f32[2048]{0:T(1024)} %param.28) | copy-start | bytes 24580
  413.1 15.2 %collective-permute-start.8 = (f32[1020,1024]{1,0:T(8,128)}, f32[1020,1024]{1,0:T(8,128)}, u32[]{:S(2)}, u32[]{:S(2)}) collective-permute-start(f32[1020,1024]{1,0:T(8,128)} %fusion.45), channel_id=1, source_target_pairs={{0,1},{1,0},{2,3},{3,2},{4,5},{5,4},{6,7},{7,6},{8,9},{9,8},{10,11... | collective-permute-start | bytes 12533768 | tf_op jit(solution)/shard_map/ppermute | solution.py:34
  421.6 17.7 %collective-permute-start.7 = (f32[1020,1024]{1,0:T(8,128)}, f32[1020,1024]{1,0:T(8,128)}, u32[]{:S(2)}, u32[]{:S(2)}) collective-permute-start(f32[1020,1024]{1,0:T(8,128)} %fusion.74), channel_id=1, source_target_pairs={{0,1},{1,0},{2,3},{3,2},{4,5},{5,4},{6,7},{7,6},{8,9},{9,8},{10,11... | collective-permute-start | bytes 12533768 | tf_op jit(solution)/shard_map/ppermute | solution.py:34
  480.2 266.6 %reduce-scatter.11.cloned.1.call-start = ((), (), s32[]{:S(2)}) async-start(), calls=%async_computation.11 | async-start | bytes 5242880 | tf_op jit(solution)/shard_map/reduce_scatter | solution.py:237
  488.6 258.8 %reduce-scatter.13.cloned.1.call-start = ((), (), s32[]{:S(2)}) async-start(), calls=%async_computation.12 | async-start | bytes 5242880 | tf_op jit(solution)/shard_map/reduce_scatter | solution.py:239
  504.6 299.1 %reduce-scatter.7.cloned.1.call-start = ((), (), s32[]{:S(2)}) async-start(), calls=%async_computation.9 | async-start | bytes 3932160 | tf_op jit(solution)/shard_map/reduce_scatter | solution.py:236
  567.1 52.1 %collective-permute-start.12 = (bf16[6,170,8,64]{1,3,2,0:T(8,128)(2,1)}, bf16[6,170,8,64]{1,3,2,0:T(8,128)(2,1)}, u32[]{:S(2)}, u32[]{:S(2)}) collective-permute-start(bf16[6,170,8,64]{1,3,2,0:T(8,128)(2,1)} %get-tuple-element.115), channel_id=1, source_target_pairs={{0,6},{2,0},{4,2},{6,4},{1,7},{3,1},{5,3},{7,5},{8,14},{10,8},{12,... | collective-permute-start | bytes 3133448 | tf_op jit(solution)/shard_map/ppermute | solution.py:51
  569.5 69.9 %collective-permute-start.14 = (bf16[6,170,8,64]{1,3,2,0:T(8,128)(2,1)}, bf16[6,170,8,64]{1,3,2,0:T(8,128)(2,1)}, u32[]{:S(2)}, u32[]{:S(2)}) collective-permute-start(bf16[6,170,8,64]{1,3,2,0:T(8,128)(2,1)} %get-tuple-element.116), channel_id=1, source_target_pairs={{0,2},{2,4},{4,6},{6,0},{1,3},{3,5},{5,7},{7,1},{8,10},{10,12},{12... | collective-permute-start | bytes 3133448 | tf_op jit(solution)/shard_map/ppermute | solution.py:51
  569.5 71.3 %collective-permute-start.13 = (bf16[6,170,8,64]{1,3,2,0:T(8,128)(2,1)}, bf16[6,170,8,64]{1,3,2,0:T(8,128)(2,1)}, u32[]{:S(2)}, u32[]{:S(2)}) collective-permute-start(bf16[6,170,8,64]{1,3,2,0:T(8,128)(2,1)} %get-tuple-element.117), channel_id=1, source_target_pairs={{0,4},{2,6},{4,0},{6,2},{1,5},{3,7},{5,1},{7,3},{8,12},{10,14},{12... | collective-permute-start | bytes 3133448 | tf_op jit(solution)/shard_map/ppermute | solution.py:51
  616.7 55.4 %collective-permute-start.9 = (bf16[6,170,8,64]{1,3,2,0:T(8,128)(2,1)}, bf16[6,170,8,64]{1,3,2,0:T(8,128)(2,1)}, u32[]{:S(2)}, u32[]{:S(2)}) collective-permute-start(bf16[6,170,8,64]{1,3,2,0:T(8,128)(2,1)} %get-tuple-element.112), channel_id=1, source_target_pairs={{0,6},{2,0},{4,2},{6,4},{1,7},{3,1},{5,3},{7,5},{8,14},{10,8},{12,... | collective-permute-start | bytes 3133448 | tf_op jit(solution)/shard_map/ppermute | solution.py:51
  618.9 87.6 %collective-permute-start.11 = (bf16[6,170,8,64]{1,3,2,0:T(8,128)(2,1)}, bf16[6,170,8,64]{1,3,2,0:T(8,128)(2,1)}, u32[]{:S(2)}, u32[]{:S(2)}) collective-permute-start(bf16[6,170,8,64]{1,3,2,0:T(8,128)(2,1)} %get-tuple-element.113), channel_id=1, source_target_pairs={{0,2},{2,4},{4,6},{6,0},{1,3},{3,5},{5,7},{7,1},{8,10},{10,12},{12... | collective-permute-start | bytes 3133448 | tf_op jit(solution)/shard_map/ppermute | solution.py:51
  619.2 88.3 %collective-permute-start.10 = (bf16[6,170,8,64]{1,3,2,0:T(8,128)(2,1)}, bf16[6,170,8,64]{1,3,2,0:T(8,128)(2,1)}, u32[]{:S(2)}, u32[]{:S(2)}) collective-permute-start(bf16[6,170,8,64]{1,3,2,0:T(8,128)(2,1)} %get-tuple-element.114), channel_id=1, source_target_pairs={{0,4},{2,6},{4,0},{6,2},{1,5},{3,7},{5,1},{7,3},{8,12},{10,14},{12... | collective-permute-start | bytes 3133448 | tf_op jit(solution)/shard_map/ppermute | solution.py:51
  645.8 61.7 %copy-start.2 = (f32[6,170,1,512]{1,3,0,2:T(8,128)S(1)}, f32[6,170,1,512]{1,3,0,2:T(8,128)}, u32[]{:S(2)}) copy-start(f32[6,170,1,512]{1,3,0,2:T(8,128)} %copy-done.1) | copy-start | bytes 6266884
  658.5 53.4 %copy-start.26 = (f32[6,170,8]{1,2,0:T(8,128)S(1)}, f32[6,170,8]{1,2,0:T(8,128)}, u32[]{:S(2)}) copy-start(f32[6,170,8]{1,2,0:T(8,128)} %copy-done.25) | copy-start | bytes 97924
  658.5 53.5 %copy-start.24 = (f32[6,170,8]{1,2,0:T(8,128)S(1)}, f32[6,170,8]{1,2,0:T(8,128)}, u32[]{:S(2)}) copy-start(f32[6,170,8]{1,2,0:T(8,128)} %copy-done.23) | copy-start | bytes 97924
  745.9 140.0 %all-gather.25.cloned.1.call-start = ((), (), s32[]{:S(2)}) async-start(), calls=%async_computation.14 | async-start | bytes 1310720 | tf_op jit(solution)/shard_map/all_gather | solution.py:242
  746.7 219.5 %all-gather.27.cloned.1.call-start = ((), (), s32[]{:S(2)}) async-start(), calls=%async_computation.15 | async-start | bytes 5242880 | tf_op jit(solution)/shard_map/all_gather | solution.py:242
  747.3 222.0 %all-gather.29.cloned.1.call-start = ((), (), s32[]{:S(2)}) async-start(), calls=%async_computation.16 | async-start | bytes 5242880 | tf_op jit(solution)/shard_map/all_gather | solution.py:242
  748.0 240.8 %all-gather.23.cloned.1.call-start = ((), (), s32[]{:S(2)}) async-start(), calls=%async_computation.13 | async-start | bytes 3932160 | tf_op jit(solution)/shard_map/all_gather | solution.py:242
  748.0 55.8 %copy-start.37 = (f32[6,1024]{1,0:T(8,128)S(1)}, f32[6,1024]{1,0:T(8,128)}, u32[]{:S(2)}) copy-start(f32[6,1024]{1,0:T(8,128)} %get-tuple-element.87) | copy-start | bytes 73732
  748.1 55.8 %copy-start.36 = (f32[6,1024]{1,0:T(8,128)S(1)}, f32[6,1024]{1,0:T(8,128)}, u32[]{:S(2)}) copy-start(f32[6,1024]{1,0:T(8,128)} %get-tuple-element.91) | copy-start | bytes 73732
  748.1 55.8 %copy-start.38 = (f32[6,1024]{1,0:T(8,128)S(1)}, f32[6,1024]{1,0:T(8,128)}, u32[]{:S(2)}) copy-start(f32[6,1024]{1,0:T(8,128)} %get-tuple-element.80) | copy-start | bytes 73732
  748.1 55.9 %copy-start.59 = (f32[8]{0:T(128)S(1)}, f32[8]{0:T(128)}, u32[]{:S(2)}) copy-start(f32[8]{0:T(128)} %param.24) | copy-start | bytes 100
  748.1 56.0 %copy-start.46 = (f32[1024]{0:T(1024)S(1)}, f32[1024]{0:T(1024)}, u32[]{:S(2)}) copy-start(f32[1024]{0:T(1024)} %get-tuple-element.94) | copy-start | bytes 12292
  748.1 56.0 %copy-start.48 = (f32[2048]{0:T(1024)S(1)}, f32[2048]{0:T(1024)}, u32[]{:S(2)}) copy-start(f32[2048]{0:T(1024)} %get-tuple-element.95) | copy-start | bytes 24580
  755.5 132.7 %collective-permute-start.15 = (f32[1020,1024]{1,0:T(8,128)}, f32[1020,1024]{1,0:T(8,128)}, u32[]{:S(2)}, u32[]{:S(2)}) collective-permute-start(f32[1020,1024]{1,0:T(8,128)} %fusion.87), channel_id=1, source_target_pairs={{0,1},{1,0},{2,3},{3,2},{4,5},{5,4},{6,7},{7,6},{8,9},{9,8},{10,11... | collective-permute-start | bytes 12533768 | tf_op jit(solution)/shard_map/ppermute | solution.py:34
  944.7 20.8 %all-to-all-start = ((f32[4,6,256]{2,1,0:T(8,128)}), f32[4,6,256]{2,1,0:T(8,128)S(1)}, u32[]{:S(2)}, u32[]{:S(2)}) async-start(f32[4,6,256]{2,1,0:T(8,128)} %fusion.88), calls=%async_computation | async-start | bytes 65536 | tf_op jit(solution)/shard_map/all_to_all | solution.py:232
  (46 other events, 469.7 us)
Sparse Core Ops, SparseCore 0:
  10.1 79.1 all-gather.14
  90.9 31.7 all-gather.16
  124.3 79.0 all-gather.18
  311.5 81.0 all-gather.20
  480.3 25.6 reduce-scatter.8
  508.1 75.2 reduce-scatter.10
  585.7 77.2 reduce-scatter.12
  746.1 57.6 reduce-scatter.6
  805.6 26.7 all-gather.24
  834.1 53.0 all-gather.26
  889.1 54.3 all-gather.28
  945.2 43.5 all-gather.22
